TPU v7x, 512 devices: a whole 4x8x8 slice. The times are simulated.
512 devices in a mesh: dp: 16 (over z, core), mp: 32 (over x, y).
Axes of the slice: x: 4, y: 8, z: 8, core: 2. Of those that a mesh axis runs over, the one named last changes fastest.
Arguments:
- tokens: bfloat16 [2048, 4096], P(('dp', 'mp')), may hold values from -6 to 6
- hidden_grad: bfloat16 [2048, 14336], P('dp', 'mp'), may hold values from -0.125 to 0.125
- gate_weight: bfloat16 [4096, 14336], P('dp', 'mp'), may hold values from -0.09375 to 0.09375
- up_weight: bfloat16 [4096, 14336], P('dp', 'mp'), may hold values from -0.09375 to 0.09375
- gate_probe: bfloat16 [4096, 14336], P('dp', 'mp'), may hold values from -1 to 1, as said below
- gate_mean: float32 [4096, 14336], P('dp', 'mp'), may hold values from -0.6 to 0.6
- gate_curve: float32 [4096, 14336], P('dp', 'mp'), may hold values from 1 to 10
- group_counts: int32 [16], replicated, may hold values from 32 to 128, as said below
Outputs:
- gate_weight_new: bfloat16 [4096, 14336], P('dp', 'mp')
- gate_mean_new: float32 [4096, 14336], P('dp', 'mp')
- gate_curve_new: float32 [4096, 14336], P('dp', 'mp')
Inputs may be any that keep to these rules, and one draw needn't show every extreme that they name: `group_counts`: some data group has exactly 128 live tokens in every draw. `gate_probe`: every entry is -1 or 1, each sign drawn independently.
All inputs are finite; a program needn't handle non-finite values.
Results may differ from a plain program's by a relative error of at most 0.0017.
Values may be sent and summed in bfloat16 or wider, within the bound.
No kernel may reach another device: no remote copies, remote signals or barrier semaphores. Data moves between devices by JAX's collectives and lax.ppermute only.
A program may use at most 64 MiB of HBM per device.

v0:
```python
import jax
import jax.numpy as jnp
from jax import lax
from jax.sharding import PartitionSpec as P

first_decay = 0.9
second_decay = 0.999
learn_rate = 0.15
epsilon_term = 0.0001
first_fix = 1.0 - 0.9**10
second_fix = 1.0 - 0.999**10


def silu_parts(inputs):
    sigmoid_part = jax.nn.sigmoid(inputs)
    silu_slope = sigmoid_part * (1.0 + inputs * (1.0 - sigmoid_part))
    silu_bend = sigmoid_part * (1.0 - sigmoid_part) * (2.0 + inputs * (1.0 - 2.0 * sigmoid_part))
    return (silu_slope, silu_bend)


def adahessian(weight, mean_old, curve_old, gradient, probe_value, product):
    diagonal = probe_value.astype(jnp.float32) * product
    mean_new = first_decay * mean_old + (1.0 - first_decay) * gradient
    curve_new = second_decay * curve_old + (1.0 - second_decay) * diagonal * diagonal
    step_ratio = mean_new / first_fix / (jnp.sqrt(curve_new / second_fix) + epsilon_term)
    weight_new = (weight.astype(jnp.float32) - learn_rate * step_ratio).astype(jnp.bfloat16)
    return (weight_new, mean_new, curve_new)


def body(
    tokens, hidden_grad, gate_weight, up_weight, gate_probe, gate_mean, gate_curve, group_counts
):
    whole = lax.all_gather(tokens, "mp", axis=0, tiled=True)
    columns = lax.all_to_all(whole, "dp", split_axis=1, concat_axis=0, tiled=True)
    group_rows = whole.shape[0]
    width = gate_weight.shape[1]
    pieces = (
        lax.all_gather(gate_weight, "dp", axis=0, tiled=True),
        lax.all_gather(up_weight, "dp", axis=0, tiled=True),
    )
    gate_pre, up_pre = tuple(
        (jnp.dot(whole, piece, preferred_element_type=jnp.float32) for piece in pieces)
    )
    selected = columns
    gate_tan = lax.psum_scatter(
        jnp.dot(selected, gate_probe, preferred_element_type=jnp.float32),
        "dp",
        scatter_dimension=0,
        tiled=True,
    )
    group_index = lax.axis_index("dp")
    limit = lax.dynamic_index_in_dim(group_counts, group_index, 0, keepdims=False)
    live = (jnp.arange(group_rows, dtype=jnp.int32) < limit).astype(jnp.float32)
    silu_slope, silu_bend = silu_parts(gate_pre)
    masked = hidden_grad.astype(jnp.float32) * live[:, None]
    grad_gate = (masked * up_pre * silu_slope).astype(jnp.bfloat16)
    tan_gate = (masked * up_pre * silu_bend * gate_tan).astype(jnp.bfloat16)
    packed = jnp.concatenate([grad_gate, tan_gate], 1)
    selected = columns
    sums = lax.dot_general(
        selected,
        lax.all_gather(packed, "dp", axis=0, tiled=True),
        (((0,), (0,)), ((), ())),
        preferred_element_type=jnp.float32,
    )
    gate_out = adahessian(
        gate_weight, gate_mean, gate_curve, sums[:, :width], gate_probe, sums[:, width:]
    )
    return (gate_out[0], gate_out[1], gate_out[2])


def solution(mesh):
    return jax.shard_map(
        body,
        mesh=mesh,
        in_specs=(
            P(("dp", "mp"), None),
            P("dp", "mp"),
            P("dp", "mp"),
            P("dp", "mp"),
            P("dp", "mp"),
            P("dp", "mp"),
            P("dp", "mp"),
            P(),
        ),
        out_specs=(P("dp", "mp"), P("dp", "mp"), P("dp", "mp")),
        check_vma=False,
    )
```

profile of v0, /device:TPU:1, one launch (start us, length us, event | category | flops | bytes accessed | tf_op | source)
XLA Modules:
  0.0 342.0 jit_solution(2087898380235495970)
XLA Ops:
  7.2 0.0 copy-start.2
  7.2 0.0 all-gather.12.cloned.1.call-start
  7.2 0.7 all-gather.12.cloned.1.call-update
  7.9 0.0 all-gather.8.cloned.1.call-start
  8.0 0.7 all-gather.8.cloned.1.call-update
  8.7 0.0 all-gather.6.cloned.1.call-start
  8.7 0.7 all-gather.6.cloned.1.call-update
  9.4 0.0 reduce-scatter.2.cloned.1.call-start
  9.4 83.9 %all-gather.12.cloned.1.call-done = bf16[32,4,4096]{2,1,0:T(4,128)(2,1)} async-done(((bf16[1,4,4096]{2,1,0:T(4,128)(2,1)}), bf16[32,4,4096]{2,1,0:T(4,128)(2,1)}) %all-gather.12.cloned.1.call-update) | async-done | bytes 1048592 | tf_op jit(solution)/shard_map/all_gather | solution.py:33
  93.3 1.8 all_to_all.14
  95.1 0.3 copy.12
  95.5 47.8 %all_to_all.19 = bf16[128,16,256]{2,0,1:T(8,128)(2,1)S(1)} all-to-all(bf16[128,16,256]{2,0,1:T(8,128)(2,1)S(1)} %copy.12), channel_id=1, replica_groups=mesh['dp'=16,'mp'=32] {'dp'}, dimensions={1} | all-to-all | bytes 2097152 | tf_op jit(solution)/shard_map/all_to_all | solution.py:34
  143.3 0.0 copy-done.2
  143.3 2.6 fusion.13
  145.9 0.0 copy-start.6
  145.9 0.0 copy-start
  145.9 0.0 reduce-scatter.2.cloned.1.call-update
  145.9 0.0 copy-start.5
  145.9 0.0 all-gather.10.cloned.1.call-start
  146.0 0.6 copy-done.6
  146.5 0.6 dynamic_slice.4
  147.1 0.6 compare_convert_fusion
  147.8 0.0 copy-done
  147.8 0.3 reshape.15
  148.1 15.2 %all-gather.8.cloned.1.call-done = bf16[4096,448]{0,1:T(8,128)(2,1)} async-done(((bf16[256,448]{0,1:T(8,128)(2,1)}), bf16[4096,448]{0,1:T(8,128)(2,1)}) %all-gather.8.cloned.1.call-update) | async-done | bytes 3670032 | tf_op jit(solution)/shard_map/all_gather | solution.py:38
  163.3 3.1 fusion.12
  166.5 45.4 %all-gather.6.cloned.1.call-done = bf16[4096,448]{0,1:T(8,128)(2,1)} async-done(((bf16[256,448]{0,1:T(8,128)(2,1)}), bf16[4096,448]{0,1:T(8,128)(2,1)}) %all-gather.6.cloned.1.call-update) | async-done | bytes 3670032 | tf_op jit(solution)/shard_map/all_gather | solution.py:39
  211.9 63.9 %reduce-scatter.2.cloned.1.call-done = f32[128,448]{0,1:T(8,128)} async-done(((f32[2048,448]{0,1:T(8,128)}), f32[128,448]{0,1:T(8,128)}) %reduce-scatter.2.cloned.1.call-update) | async-done | bytes 229392 | tf_op jit(solution)/shard_map/reduce_scatter | solution.py:45
  275.8 0.0 copy-done.5
  275.8 3.2 fusion.5
  278.9 0.7 pad_maximum_fusion
  279.6 0.0 all-gather.10.cloned.1.call-update
  279.7 0.0 copy-start.1
  279.7 0.0 copy-start.3
  279.7 0.0 copy-start.4
  279.7 51.3 %all-gather.10.cloned.1.call-done = bf16[2048,896]{0,1:T(8,128)(2,1)} async-done(((bf16[128,896]{0,1:T(8,128)(2,1)}), bf16[2048,896]{0,1:T(8,128)(2,1)}) %all-gather.10.cloned.1.call-update) | async-done | bytes 3670032 | tf_op jit(solution)/shard_map/all_gather | solution.py:62
  331.0 3.1 convolution_bitcast_fusion
  334.2 0.0 copy-done.1
  334.2 0.0 copy-done.3
  334.2 0.0 copy-done.4
  334.2 1.2 subtract_convert_fusion
Async XLA Ops:
  7.2 136.1 %copy-start.2 = (bf16[256,448]{0,1:T(8,128)(2,1)S(1)}, bf16[256,448]{0,1:T(8,128)(2,1)}, u32[]{:S(2)}) copy-start(bf16[256,448]{0,1:T(8,128)(2,1)} %param.12) | copy-start | bytes 688132
  7.2 86.2 %all-gather.12.cloned.1.call-start = ((), (), s32[]{:S(2)}) async-start(), calls=%async_computation.6 | async-start | bytes 1081344 | tf_op jit(solution)/shard_map/all_gather | solution.py:33
  7.9 155.4 %all-gather.8.cloned.1.call-start = ((), (), s32[]{:S(2)}) async-start(), calls=%async_computation.3 | async-start | bytes 3899392 | tf_op jit(solution)/shard_map/all_gather | solution.py:38
  8.7 203.2 %all-gather.6.cloned.1.call-start = ((), (), s32[]{:S(2)}) async-start(), calls=%async_computation.2 | async-start | bytes 3899392 | tf_op jit(solution)/shard_map/all_gather | solution.py:39
  9.4 266.4 %reduce-scatter.2.cloned.1.call-start = ((), (), s32[]{:S(2)}) async-start(), calls=%async_computation.4 | async-start | bytes 3899392 | tf_op jit(solution)/shard_map/reduce_scatter | solution.py:45
  145.9 0.7 copy-start.6
  145.9 1.9 copy-start
  145.9 129.9 %copy-start.5 = (bf16[128,448]{0,1:T(8,128)(2,1)S(1)}, bf16[128,448]{0,1:T(8,128)(2,1)}, u32[]{:S(2)}) copy-start(bf16[128,448]{0,1:T(8,128)(2,1)} %param.9) | copy-start | bytes 344068
  145.9 185.1 %all-gather.10.cloned.1.call-start = ((), (), s32[]{:S(2)}) async-start(), calls=%async_computation.5 | async-start | bytes 3899392 | tf_op jit(solution)/shard_map/all_gather | solution.py:62
  279.7 54.5 %copy-start.1 = (bf16[256,448]{0,1:T(8,128)(2,1)S(1)}, bf16[256,448]{0,1:T(8,128)(2,1)}, u32[]{:S(2)}) copy-start(bf16[256,448]{0,1:T(8,128)(2,1)} %param.10) | copy-start | bytes 688132
  279.7 54.5 %copy-start.3 = (f32[256,448]{0,1:T(8,128)S(1)}, f32[256,448]{0,1:T(8,128)}, u32[]{:S(2)}) copy-start(f32[256,448]{0,1:T(8,128)} %param.13) | copy-start | bytes 1376260
  279.7 54.5 %copy-start.4 = (f32[256,448]{0,1:T(8,128)S(1)}, f32[256,448]{0,1:T(8,128)}, u32[]{:S(2)}) copy-start(f32[256,448]{0,1:T(8,128)} %param.14) | copy-start | bytes 1376260
Sparse Core Ops, SparseCore 0:
  11.2 82.1 all-gather.11
  95.4 67.8 all-gather.7
  165.4 46.4 all-gather.5
  214.6 61.1 reduce-scatter.1
  279.8 51.2 all-gather.9
where the time goes:
time: 342 us
  waiting for transfers between devices  262 us (77%)
  blocking collectives  47.8 us (14%)
  between operations  13.9 us (4%)
  matrix products  12 us (4%)
  local copies, waits for them, and re-layouts  3.58 us (1%)
    all_gather x1, waiting for transfers between devices, body(): whole = lax.all_gather(tokens, 'mp', axis=0, tiled=True)  83.9 us
    reduce_scatter x1, waiting for transfers between devices, body(): lax.psum_scatter(jnp.dot(selected, gate_probe, preferred_element_type=jnp...  63.9 us
    all_gather x1, waiting for transfers between devices, body(): lax.all_gather(packed, 'dp', axis=0, tiled=True)  51.3 us
    all_to_all x1, blocking collectives, body(): lax.all_to_all(whole, 'dp', split_axis=1, concat_axis=0, tiled=True)  47.8 us
    all_gather x1, waiting for transfers between devices, body(): lax.all_gather(up_weight, 'dp', axis=0, tiled=True)  45.4 us
    all_gather x1, waiting for transfers between devices, body(): lax.all_gather(gate_weight, 'dp', axis=0, tiled=True)  15.2 us
  transfers between devices with their start and end apart: 5, of which 5 were waited for; matrix products, arithmetic and copies ran while one was open for 2% of the time, Pallas kernels for 0%

commit v1 on v0

--- a/solution.py
+++ b/solution.py
@@ -9,6 +9,19 @@
 epsilon_term = 0.0001
 first_fix = 1.0 - 0.9**10
 second_fix = 1.0 - 0.999**10
+
+
+def gather_around(value, axis, dim):
+    ways = lax.axis_size(axis)
+    up = [(d, (d + 1) % ways) for d in range(ways)]
+    down = [(d, (d - 1) % ways) for d in range(ways)]
+    earlier, later = ([value], [value])
+    for _ in range(ways // 2):
+        earlier.append(lax.ppermute(earlier[-1], axis, up))
+    for _ in range((ways - 1) // 2):
+        later.append(lax.ppermute(later[-1], axis, down))
+    line = jnp.concatenate([*earlier[::-1], *later[1:]], axis=dim)
+    return jnp.roll(line, (lax.axis_index(axis) - ways // 2) * value.shape[dim], axis=dim)
 
 
 def silu_parts(inputs):
@@ -36,7 +49,7 @@
     width = gate_weight.shape[1]
     pieces = (
         lax.all_gather(gate_weight, "dp", axis=0, tiled=True),
-        lax.all_gather(up_weight, "dp", axis=0, tiled=True),
+        gather_around(up_weight, "dp", 0),
     )
     gate_pre, up_pre = tuple(
         (jnp.dot(whole, piece, preferred_element_type=jnp.float32) for piece in pieces)

time: 342 us -> 306 us (0.89)
  waiting for transfers between devices: 262 us -> 160 us
  local copies, waits for them, and re-layouts: 3.58 us -> 40 us
  starting transfers between devices: 0.19 us -> 27.3 us
    reduce_scatter x1, waiting for transfers between devices: 63.9 us -> 0.02 us  [body(): lax.psum_scatter(jnp.dot(selected, gate_probe, preferred_element_type=jnp...]
    all_gather x1 -> x0, waiting for transfers between devices: 45.4 us -> none  [body(): lax.all_gather(up_weight, 'dp', axis=0, tiled=True)]
    unnamed x15 -> x66, local copies, waits for them, and re-layouts: 0.88 us -> 36.6 us
    ppermute x0 -> x15, starting transfers between devices: none -> 27.2 us  [the longest x8 17 us: gather_around(): earlier.append(lax.ppermute(earlier[-1], axis, up))]
    ppermute x0 -> x15, waiting for transfers between devices: none -> 23.5 us  [the longest x8 19.2 us: gather_around(): earlier.append(lax.ppermute(earlier[-1], axis, up))]
    all_gather x1, waiting for transfers between devices: 15.2 us -> 0.02 us  [body(): lax.all_gather(gate_weight, 'dp', axis=0, tiled=True)]
  transfers between devices with their start and end apart: 5 -> 19, of which waited for: 5 -> 11; matrix products, arithmetic and copies ran while one was open for 2% -> 15% of each run, Pallas kernels for 0% -> 0%
where the time goes in v1:
time: 306 us
  waiting for transfers between devices  160 us (52%)
  blocking collectives  47.9 us (16%)
  local copies, waits for them, and re-layouts  40 us (13%)
  starting transfers between devices  27.3 us (9%)
  between operations  14 us (5%)
  matrix products  13.9 us (5%)
    all_gather x1, waiting for transfers between devices, body(): whole = lax.all_gather(tokens, 'mp', axis=0, tiled=True)  84.6 us
    all_gather x1, waiting for transfers between devices, body(): lax.all_gather(packed, 'dp', axis=0, tiled=True)  50.5 us
    all_to_all x1, blocking collectives, body(): lax.all_to_all(whole, 'dp', split_axis=1, concat_axis=0, tiled=True)  47.9 us
    unnamed x66, local copies, waits for them, and re-layouts  36.6 us
    ppermute x8, waiting for transfers between devices, gather_around(): earlier.append(lax.ppermute(earlier[-1], axis, up))  19.2 us
    ppermute x8, starting transfers between devices, gather_around(): earlier.append(lax.ppermute(earlier[-1], axis, up))  17 us
    ppermute x7, starting transfers between devices, gather_around(): later.append(lax.ppermute(later[-1], axis, down))  10.2 us
    dot_general x2, matrix products, body(): jnp.dot(whole, piece, preferred_element_type=jnp.float32)  7.26 us
  transfers between devices with their start and end apart: 19, of which 11 were waited for; matrix products, arithmetic and copies ran while one was open for 15% of the time, Pallas kernels for 0%

profile of v1, /device:TPU:1, one launch (start us, length us, event | category | flops | bytes accessed | tf_op | source)
XLA Modules:
  0.0 305.8 jit_solution(3724857919400656464)
XLA Ops:
  7.2 0.7 all-gather.9.cloned.1.call-update
  7.9 0.7 all-gather.5.cloned.1.call-update
  8.7 84.6 %all-gather.9.cloned.1.call-done = bf16[32,4,4096]{2,1,0:T(4,128)(2,1)} async-done(((bf16[1,4,4096]{2,1,0:T(4,128)(2,1)}), bf16[32,4,4096]{2,1,0:T(4,128)(2,1)}) %all-gather.9.cloned.1.call-update) | async-done | bytes 1048592 | tf_op jit(solution)/shard_map/all_gather | solution.py:46
  93.3 1.8 all_to_all.14
  95.5 47.9 %all_to_all.19 = bf16[128,16,256]{2,0,1:T(8,128)(2,1)S(1)} all-to-all(bf16[128,16,256]{2,0,1:T(8,128)(2,1)S(1)} %copy.12), channel_id=1, replica_groups=mesh['dp'=16,'mp'=32] {'dp'}, dimensions={1} | all-to-all | bytes 2097152 | tf_op jit(solution)/shard_map/all_to_all | solution.py:47
  143.4 3.5 %fusion.22 = f32[2048,448]{0,1:T(8,128)} fusion(bf16[2048,256]{1,0:T(8,128)(2,1)S(1)} %bitcast.18, bf16[256,448]{0,1:T(8,128)(2,1)} %param.12), kind=kOutput, calls=%fused_computation.58 | convolution fusion | flops 469762048 | bytes 4947968 | tf_op jit(solution)/shard_map/dot_general | solution.py:59
  147.1 4.9 %collective-permute-done = bf16[256,448]{0,1:T(8,128)(2,1)S(1)} collective-permute-done((bf16[256,448]{0,1:T(8,128)(2,1)S(1)}, bf16[256,448]{0,1:T(8,128)(2,1)S(1)}, u32[]{:S(2)}, u32[]{:S(2)}) %collective-permute-start) | collective-permute-done | bytes 229408 | tf_op jit(solution)/shard_map/ppermute | solution.py:20
  152.0 2.5 collective-permute-start.1
  154.4 6.5 %collective-permute-done.1 = bf16[256,448]{0,1:T(8,128)(2,1)S(1)} collective-permute-done((bf16[256,448]{0,1:T(8,128)(2,1)S(1)}, bf16[256,448]{0,1:T(8,128)(2,1)S(1)}, u32[]{:S(2)}, u32[]{:S(2)}) %collective-permute-start.1) | collective-permute-done | bytes 229408 | tf_op jit(solution)/shard_map/ppermute | solution.py:20
  160.9 2.5 collective-permute-start.2
  163.4 3.0 collective-permute-done.2
  166.4 2.5 collective-permute-start.3
  168.9 3.0 collective-permute-done.3
  171.8 2.5 collective-permute-start.4
  174.3 0.7 copy-done.2
  175.6 1.7 collective-permute-done.4
  177.3 2.5 collective-permute-start.5
  179.8 0.9 collective-permute-done.11
  180.7 0.7 copy-done.4
  181.4 2.0 collective-permute-start.12
  183.5 2.6 collective-permute-start.6
  186.1 2.0 collective-permute-done.12
  188.2 3.7 %collective-permute-start.13 = (bf16[256,448]{0,1:T(8,128)(2,1)}, bf16[256,448]{0,1:T(8,128)(2,1)}, u32[]{:S(2)}, u32[]{:S(2)}) collective-permute-start(bf16[256,448]{0,1:T(8,128)(2,1)} %collective-permute-done.12), channel_id=1, source_target_pairs={{0,480},{32,0},{64,32},{96,64},{128,96},{160,128},{192,160},{224,1... | collective-permute-start | bytes 688136 | tf_op jit(solution)/shard_map/ppermute | solution.py:22
  191.9 2.0 collective-permute-start.7
  195.1 1.4 collective-permute-done.13
  196.5 3.9 %collective-permute-start.14 = (bf16[256,448]{0,1:T(8,128)(2,1)}, bf16[256,448]{0,1:T(8,128)(2,1)S(1)}, u32[]{:S(2)}, u32[]{:S(2)}) collective-permute-start(bf16[256,448]{0,1:T(8,128)(2,1)} %collective-permute-done.13), channel_id=1, source_target_pairs={{0,480},{32,0},{64,32},{96,64},{128,96},{160,128},{192,160},{224,1... | collective-permute-start | bytes 688136 | tf_op jit(solution)/shard_map/ppermute | solution.py:22
  200.4 1.7 constant_dynamic-update-slice_fusion.31
  202.1 1.7 constant_dynamic-update-slice_fusion.30
  203.7 1.7 constant_dynamic-update-slice_fusion.29
  205.4 1.7 constant_dynamic-update-slice_fusion.28
  207.1 1.7 constant_dynamic-update-slice_fusion.27
  208.8 0.7 constant_dynamic-update-slice_fusion.26
  209.5 0.7 constant_dynamic-update-slice_fusion.25
  210.2 0.7 constant_dynamic-update-slice_fusion.24
  210.9 0.7 constant_dynamic-update-slice_fusion.23
  211.6 0.7 constant_dynamic-update-slice_fusion.22
  212.4 0.7 constant_dynamic-update-slice_fusion.21
  213.1 1.7 constant_dynamic-update-slice_fusion.20
  214.8 1.7 constant_dynamic-update-slice_fusion.19
  216.4 1.7 constant_dynamic-update-slice_fusion.18
  218.1 1.7 constant_dynamic-update-slice_fusion.17
  219.8 0.7 constant_dynamic-update-slice_fusion.16
  220.5 1.7 constant_dynamic-update-slice_fusion.15
  222.1 1.7 constant_dynamic-update-slice_fusion.14
  223.8 0.7 constant_dynamic-update-slice_fusion.13
  224.5 0.7 constant_dynamic-update-slice_fusion.12
  225.3 0.7 constant_dynamic-update-slice_fusion.11
  226.0 0.7 constant_dynamic-update-slice_fusion.10
  226.7 0.7 constant_dynamic-update-slice_fusion.9
  227.5 0.8 constant_dynamic-update-slice_fusion.8
  228.3 0.7 constant_dynamic-update-slice_fusion.7
  229.0 0.8 constant_dynamic-update-slice_fusion.6
  229.7 0.7 constant_dynamic-update-slice_fusion.5
  230.5 0.7 constant_dynamic-update-slice_fusion.4
  231.2 0.7 constant_dynamic-update-slice_fusion.3
  231.9 1.7 constant_dynamic-update-slice_fusion.2
  233.6 1.7 constant_dynamic-update-slice_fusion.1
  235.3 0.7 constant_dynamic-update-slice_fusion
  236.3 3.8 %fusion.21 = f32[128,448]{0,1:T(8,128)} fusion(bf16[128,4096]{1,0:T(8,128)(2,1)S(1)} %reshape.15, bf16[4096,448]{0,1:T(8,128)(2,1)} %all-gather.5.cloned.1.call-done), kind=kOutput, calls=%fused_computation.57 | convolution fusion | flops 469762048 | bytes 4947968 | tf_op jit(solution)/shard_map/dot_general | solution.py:55
  240.2 3.4 %fusion.13 = (bf16[128,448]{0,1:T(8,128)(2,1)S(1)}, bf16[128,448]{0,1:T(8,128)(2,1)S(1)}) fusion(f32[128,448]{0,1:T(8,128)} %fusion.21, f32[128,448]{0,1:T(8,128)} %reduce-scatter.2.cloned.1.call-done, bf16[128,4096]{1,0:T(8,128)(2,1)S(1)} %reshape.15, bf16[8192,448]{0,1:T(8,128)(2,1)} %constant_dynamic-update-slice_fusion, s32[]{:T(128)S(6)} %select_n.19, ...), kind=kOutput, calls=%fused_computation.16 | convolution fusion | flops 470966272 | bytes 5521924 | tf_op jit(solution)/shard_map/dot_general | solution.py:55
  243.6 0.7 pad_maximum_fusion
  244.4 50.5 %all-gather.7.cloned.1.call-done = bf16[2048,896]{0,1:T(8,128)(2,1)} async-done(((bf16[128,896]{0,1:T(8,128)(2,1)}), bf16[2048,896]{0,1:T(8,128)(2,1)}) %all-gather.7.cloned.1.call-update) | async-done | bytes 3670032 | tf_op jit(solution)/shard_map/all_gather | solution.py:75
  294.8 3.1 %convolution_bitcast_fusion = f32[256,896]{0,1:T(8,128)S(1)} fusion(bf16[2048,896]{0,1:T(8,128)(2,1)} %all-gather.7.cloned.1.call-done, bf16[2048,256]{1,0:T(8,128)(2,1)S(1)} %bitcast.19), kind=kOutput, calls=%fused_computation.2 | convolution fusion | flops 939524096 | bytes 5636096 | tf_op jit(solution)/shard_map/dot_general | solution.py:73
  298.0 1.2 subtract_convert_fusion
  (56 shorter events, 2.9 us)
Async XLA Ops:
  7.2 86.2 %all-gather.9.cloned.1.call-start = ((), (), s32[]{:S(2)}) async-start(), calls=%async_computation.5 | async-start | bytes 1081344 | tf_op jit(solution)/shard_map/all_gather | solution.py:46
  7.9 228.4 %all-gather.5.cloned.1.call-start = ((), (), s32[]{:S(2)}) async-start(), calls=%async_computation.2 | async-start | bytes 3899392 | tf_op jit(solution)/shard_map/all_gather | solution.py:51
  8.6 231.6 %reduce-scatter.2.cloned.1.call-start = ((), (), s32[]{:S(2)}) async-start(), calls=%async_computation.3 | async-start | bytes 3899392 | tf_op jit(solution)/shard_map/reduce_scatter | solution.py:58
  95.5 51.6 %copy-start.1 = (bf16[256,448]{0,1:T(8,128)(2,1)S(1)}, bf16[256,448]{0,1:T(8,128)(2,1)}, u32[]{:S(2)}) copy-start(bf16[256,448]{0,1:T(8,128)(2,1)} %param.11) | copy-start | bytes 688132
  95.5 98.4 %copy-start.16 = (s32[16]{0:T(128)S(1)}, s32[16]{0:T(128)}, u32[]{:S(2)}) copy-start(s32[16]{0:T(128)} %param.15) | copy-start | bytes 196
  147.0 147.9 %all-gather.7.cloned.1.call-start = ((), (), s32[]{:S(2)}) async-start(), calls=%async_computation.4 | async-start | bytes 3899392 | tf_op jit(solution)/shard_map/all_gather | solution.py:75
  147.0 4.9 %collective-permute-start = (bf16[256,448]{0,1:T(8,128)(2,1)S(1)}, bf16[256,448]{0,1:T(8,128)(2,1)S(1)}, u32[]{:S(2)}, u32[]{:S(2)}) collective-permute-start(bf16[256,448]{0,1:T(8,128)(2,1)S(1)} %copy-done.1), channel_id=1, source_target_pairs={{0,32},{32,64},{64,96},{96,128},{128,160},{160,192},{192,224},{224... | collective-permute-start | bytes 688136 | tf_op jit(solution)/shard_map/ppermute | solution.py:20
  152.0 9.0 %collective-permute-start.1 = (bf16[256,448]{0,1:T(8,128)(2,1)S(1)}, bf16[256,448]{0,1:T(8,128)(2,1)S(1)}, u32[]{:S(2)}, u32[]{:S(2)}) collective-permute-start(bf16[256,448]{0,1:T(8,128)(2,1)S(1)} %collective-permute-done), channel_id=1, source_target_pairs={{0,32},{32,64},{64,96},{96,128},{128,160},{160,192},{192,224},{224... | collective-permute-start | bytes 688136 | tf_op jit(solution)/shard_map/ppermute | solution.py:20
  154.4 9.0 %collective-permute-start.8 = (bf16[256,448]{0,1:T(8,128)(2,1)S(1)}, bf16[256,448]{0,1:T(8,128)(2,1)S(1)}, u32[]{:S(2)}, u32[]{:S(2)}) collective-permute-start(bf16[256,448]{0,1:T(8,128)(2,1)S(1)} %copy-done.1), channel_id=1, source_target_pairs={{0,480},{32,0},{64,32},{96,64},{128,96},{160,128},{192,160},{224,1... | collective-permute-start | bytes 688136 | tf_op jit(solution)/shard_map/ppermute | solution.py:22
  160.9 5.4 %collective-permute-start.2 = (bf16[256,448]{0,1:T(8,128)(2,1)S(1)}, bf16[256,448]{0,1:T(8,128)(2,1)S(1)}, u32[]{:S(2)}, u32[]{:S(2)}) collective-permute-start(bf16[256,448]{0,1:T(8,128)(2,1)S(1)} %collective-permute-done.1), channel_id=1, source_target_pairs={{0,32},{32,64},{64,96},{96,128},{128,160},{160,192},{192,224},{224... | collective-permute-start | bytes 688136 | tf_op jit(solution)/shard_map/ppermute | solution.py:20
  163.4 5.4 %collective-permute-start.9 = (bf16[256,448]{0,1:T(8,128)(2,1)S(1)}, bf16[256,448]{0,1:T(8,128)(2,1)S(1)}, u32[]{:S(2)}, u32[]{:S(2)}) collective-permute-start(bf16[256,448]{0,1:T(8,128)(2,1)S(1)} %collective-permute-done.8), channel_id=1, source_target_pairs={{0,480},{32,0},{64,32},{96,64},{128,96},{160,128},{192,160},{224,1... | collective-permute-start | bytes 688136 | tf_op jit(solution)/shard_map/ppermute | solution.py:22
  166.4 5.4 %collective-permute-start.3 = (bf16[256,448]{0,1:T(8,128)(2,1)S(1)}, bf16[256,448]{0,1:T(8,128)(2,1)S(1)}, u32[]{:S(2)}, u32[]{:S(2)}) collective-permute-start(bf16[256,448]{0,1:T(8,128)(2,1)S(1)} %collective-permute-done.2), channel_id=1, source_target_pairs={{0,32},{32,64},{64,96},{96,128},{128,160},{160,192},{192,224},{224... | collective-permute-start | bytes 688136 | tf_op jit(solution)/shard_map/ppermute | solution.py:20
  168.9 5.4 %collective-permute-start.10 = (bf16[256,448]{0,1:T(8,128)(2,1)S(1)}, bf16[256,448]{0,1:T(8,128)(2,1)S(1)}, u32[]{:S(2)}, u32[]{:S(2)}) collective-permute-start(bf16[256,448]{0,1:T(8,128)(2,1)S(1)} %collective-permute-done.9), channel_id=1, source_target_pairs={{0,480},{32,0},{64,32},{96,64},{128,96},{160,128},{192,160},{224,1... | collective-permute-start | bytes 688136 | tf_op jit(solution)/shard_map/ppermute | solution.py:22
  171.8 16.4 %copy-start.6 = (bf16[256,448]{0,1:T(8,128)(2,1)}, bf16[256,448]{0,1:T(8,128)(2,1)S(1)}, u32[]{:S(2)}) copy-start(bf16[256,448]{0,1:T(8,128)(2,1)S(1)} %collective-permute-done.3) | copy-start | bytes 688132
  171.8 5.4 %collective-permute-start.4 = (bf16[256,448]{0,1:T(8,128)(2,1)S(1)}, bf16[256,448]{0,1:T(8,128)(2,1)S(1)}, u32[]{:S(2)}, u32[]{:S(2)}) collective-permute-start(bf16[256,448]{0,1:T(8,128)(2,1)S(1)} %collective-permute-done.3), channel_id=1, source_target_pairs={{0,32},{32,64},{64,96},{96,128},{128,160},{160,192},{192,224},{224... | collective-permute-start | bytes 688136 | tf_op jit(solution)/shard_map/ppermute | solution.py:20
  174.3 0.7 copy-start.2
  175.0 5.7 %collective-permute-start.11 = (bf16[256,448]{0,1:T(8,128)(2,1)S(1)}, bf16[256,448]{0,1:T(8,128)(2,1)S(1)}, u32[]{:S(2)}, u32[]{:S(2)}) collective-permute-start(bf16[256,448]{0,1:T(8,128)(2,1)S(1)} %collective-permute-done.10), channel_id=1, source_target_pairs={{0,480},{32,0},{64,32},{96,64},{128,96},{160,128},{192,160},{224,1... | collective-permute-start | bytes 688136 | tf_op jit(solution)/shard_map/ppermute | solution.py:22
  177.3 14.6 %copy-start.8 = (bf16[256,448]{0,1:T(8,128)(2,1)}, bf16[256,448]{0,1:T(8,128)(2,1)S(1)}, u32[]{:S(2)}) copy-start(bf16[256,448]{0,1:T(8,128)(2,1)S(1)} %collective-permute-done.4) | copy-start | bytes 688132
  177.3 6.3 %collective-permute-start.5 = (bf16[256,448]{0,1:T(8,128)(2,1)S(1)}, bf16[256,448]{0,1:T(8,128)(2,1)S(1)}, u32[]{:S(2)}, u32[]{:S(2)}) collective-permute-start(bf16[256,448]{0,1:T(8,128)(2,1)S(1)} %collective-permute-done.4), channel_id=1, source_target_pairs={{0,32},{32,64},{64,96},{96,128},{128,160},{160,192},{192,224},{224... | collective-permute-start | bytes 688136 | tf_op jit(solution)/shard_map/ppermute | solution.py:20
  180.7 0.7 copy-start.4
  181.4 6.8 %collective-permute-start.12 = (bf16[256,448]{0,1:T(8,128)(2,1)S(1)}, bf16[256,448]{0,1:T(8,128)(2,1)}, u32[]{:S(2)}, u32[]{:S(2)}) collective-permute-start(bf16[256,448]{0,1:T(8,128)(2,1)S(1)} %collective-permute-done.11), channel_id=1, source_target_pairs={{0,480},{32,0},{64,32},{96,64},{128,96},{160,128},{192,160},{224,1... | collective-permute-start | bytes 688136 | tf_op jit(solution)/shard_map/ppermute | solution.py:22
  183.5 8.3 %copy-start.10 = (bf16[256,448]{0,1:T(8,128)(2,1)}, bf16[256,448]{0,1:T(8,128)(2,1)S(1)}, u32[]{:S(2)}) copy-start(bf16[256,448]{0,1:T(8,128)(2,1)S(1)} %collective-permute-done.5) | copy-start | bytes 688132
  183.5 8.3 %collective-permute-start.6 = (bf16[256,448]{0,1:T(8,128)(2,1)S(1)}, bf16[256,448]{0,1:T(8,128)(2,1)}, u32[]{:S(2)}, u32[]{:S(2)}) collective-permute-start(bf16[256,448]{0,1:T(8,128)(2,1)S(1)} %collective-permute-done.5), channel_id=1, source_target_pairs={{0,32},{32,64},{64,96},{96,128},{128,160},{160,192},{192,224},{224... | collective-permute-start | bytes 688136 | tf_op jit(solution)/shard_map/ppermute | solution.py:20
  188.2 8.3 %collective-permute-start.13 = (bf16[256,448]{0,1:T(8,128)(2,1)}, bf16[256,448]{0,1:T(8,128)(2,1)}, u32[]{:S(2)}, u32[]{:S(2)}) collective-permute-start(bf16[256,448]{0,1:T(8,128)(2,1)} %collective-permute-done.12), channel_id=1, source_target_pairs={{0,480},{32,0},{64,32},{96,64},{128,96},{160,128},{192,160},{224,1... | collective-permute-start | bytes 688136 | tf_op jit(solution)/shard_map/ppermute | solution.py:22
  191.9 8.5 %collective-permute-start.7 = (bf16[256,448]{0,1:T(8,128)(2,1)}, bf16[256,448]{0,1:T(8,128)(2,1)}, u32[]{:S(2)}, u32[]{:S(2)}) collective-permute-start(bf16[256,448]{0,1:T(8,128)(2,1)} %collective-permute-done.6), channel_id=1, source_target_pairs={{0,32},{32,64},{64,96},{96,128},{128,160},{160,192},{192,224},{224... | collective-permute-start | bytes 688136 | tf_op jit(solution)/shard_map/ppermute | solution.py:20
  193.9 30.0 %copy-start.11 = (bf16[256,448]{0,1:T(8,128)(2,1)S(1)}, bf16[256,448]{0,1:T(8,128)(2,1)}, u32[]{:S(2)}) copy-start(bf16[256,448]{0,1:T(8,128)(2,1)} %copy-done.10) | copy-start | bytes 688132
  193.9 30.7 %copy-start.9 = (bf16[256,448]{0,1:T(8,128)(2,1)S(1)}, bf16[256,448]{0,1:T(8,128)(2,1)}, u32[]{:S(2)}) copy-start(bf16[256,448]{0,1:T(8,128)(2,1)} %copy-done.8) | copy-start | bytes 688132
  193.9 31.4 %copy-start.7 = (bf16[256,448]{0,1:T(8,128)(2,1)S(1)}, bf16[256,448]{0,1:T(8,128)(2,1)}, u32[]{:S(2)}) copy-start(bf16[256,448]{0,1:T(8,128)(2,1)} %copy-done.6) | copy-start | bytes 688132
  193.9 36.6 %copy-start.3 = (bf16[256,448]{0,1:T(8,128)(2,1)S(1)}, bf16[256,448]{0,1:T(8,128)(2,1)}, u32[]{:S(2)}) copy-start(bf16[256,448]{0,1:T(8,128)(2,1)} %copy-done.2) | copy-start | bytes 688132
  193.9 37.3 %copy-start.5 = (bf16[256,448]{0,1:T(8,128)(2,1)S(1)}, bf16[256,448]{0,1:T(8,128)(2,1)}, u32[]{:S(2)}) copy-start(bf16[256,448]{0,1:T(8,128)(2,1)} %copy-done.4) | copy-start | bytes 688132
  195.1 41.0 %copy-start = (bf16[32,4,4096]{2,1,0:T(4,128)(2,1)S(1)}, bf16[32,4,4096]{2,1,0:T(4,128)(2,1)}, u32[]{:S(2)}) copy-start(bf16[32,4,4096]{2,1,0:T(4,128)(2,1)} %all-gather.9.cloned.1.call-done) | copy-start | bytes 3145732
  196.5 23.3 %collective-permute-start.14 = (bf16[256,448]{0,1:T(8,128)(2,1)}, bf16[256,448]{0,1:T(8,128)(2,1)S(1)}, u32[]{:S(2)}, u32[]{:S(2)}) collective-permute-start(bf16[256,448]{0,1:T(8,128)(2,1)} %collective-permute-done.13), channel_id=1, source_target_pairs={{0,480},{32,0},{64,32},{96,64},{128,96},{160,128},{192,160},{224,1... | collective-permute-start | bytes 688136 | tf_op jit(solution)/shard_map/ppermute | solution.py:22
  240.2 57.8 %copy-start.12 = (bf16[256,448]{0,1:T(8,128)(2,1)S(1)}, bf16[256,448]{0,1:T(8,128)(2,1)}, u32[]{:S(2)}) copy-start(bf16[256,448]{0,1:T(8,128)(2,1)} %param.10) | copy-start | bytes 688132
  240.2 57.8 %copy-start.13 = (bf16[256,448]{0,1:T(8,128)(2,1)S(1)}, bf16[256,448]{0,1:T(8,128)(2,1)}, u32[]{:S(2)}) copy-start(bf16[256,448]{0,1:T(8,128)(2,1)} %param.12) | copy-start | bytes 688132
  240.2 57.8 %copy-start.14 = (f32[256,448]{0,1:T(8,128)S(1)}, f32[256,448]{0,1:T(8,128)}, u32[]{:S(2)}) copy-start(f32[256,448]{0,1:T(8,128)} %param.13) | copy-start | bytes 1376260
  240.2 57.9 %copy-start.15 = (f32[256,448]{0,1:T(8,128)S(1)}, f32[256,448]{0,1:T(8,128)}, u32[]{:S(2)}) copy-start(f32[256,448]{0,1:T(8,128)} %param.14) | copy-start | bytes 1376260
Sparse Core Ops, SparseCore 0:
  11.1 82.1 all-gather.8
  95.4 70.1 all-gather.4
  168.4 63.4 reduce-scatter.1
  244.5 50.3 all-gather.6
